TPU v7x, 32 devices: a whole 2x2x4 slice. The times are simulated.
32 devices in a mesh: groups: 2 (over y), cols: 4 (over z), slab: 2 (over x), rep: 2 (over core).
Axes of the slice: x: 2, y: 2, z: 4, core: 2. Of those that a mesh axis runs over, the one named last changes fastest.
Arguments:
- fields: bfloat16 [16, 8, 2048, 512], P('cols', 'groups', 'rep', 'slab'), parts along dimension 1, may hold values from -250 to 250
- stresses: bfloat16 [6, 8, 512, 128], P(None, 'groups', 'rep', 'slab'), parts along dimension 1, may hold values from -750 to 750
- planes: int32 [8], P('groups'), parts along dimension 0, may hold values from 0 to 2047, as said below
- active_masks: int32 [3, 6, 256], replicated, may hold values 0 or 1
Outputs:
- coefficients: float32 [3, 12, 256], P(None, 'groups', 'cols'), parts along dimension 1
- misfit: bfloat16 [6, 8, 512, 128], P(None, 'groups', 'rep', 'slab'), parts along dimension 1
There are 2 independent parts, one for each index of `groups`. A program takes and returns all parts, laid end to end along the dimension named above; an argument that names none is the same for every part. Nothing has to cross between parts.
Inputs may be any that keep to these rules, and one draw needn't show every extreme that they name: `planes`: sorted and distinct; either the first is 0 or the last is 2047.
All inputs are finite; a program needn't handle non-finite values.
Results may differ from a plain program's by a relative error of at most 0.0069.
Values may be sent and summed in bfloat16 or wider, within the bound.
No kernel may reach another device: no remote copies, remote signals or barrier semaphores. Data moves between devices by JAX's collectives and lax.ppermute only.
A program may use at most 128 MiB of HBM per device.

v0:
```python
import math
import jax
import jax.numpy as jnp
import numpy as np
from jax import lax
from jax.sharding import PartitionSpec as P

STRESS = 6
TERMS = 256
NY = 2048
PASSES = 3
ITERS = 3
ridge_weight = 0.05
epsilon = 1e-06


def extended(array, sides, width):
    for axis, dim in sides:
        count, length = (lax.axis_size(axis), array.shape[dim])
        up = [(i, (i + 1) % count) for i in range(count)]
        down = [(j, i) for i, j in up]
        last = lax.slice_in_dim(array, length - width, length, axis=dim)
        leading = lax.slice_in_dim(array, 0, width, axis=dim)
        before = lax.ppermute(last, axis, up)
        after = lax.ppermute(leading, axis, down)
        array = jnp.concatenate([before, array, after], axis=dim)
    return array


def tree_sum(value, axes):
    for axis in axes:
        count = lax.axis_size(axis)
        if count & count - 1:
            value = lax.psum(value, axis)
            continue
        step = 1
        while step < count:
            partner = [(i, i ^ step) for i in range(count)]
            value = value + lax.ppermute(value, axis, partner)
            step *= 2
    return value


def kernel(spread):
    offsets = np.arange(13) - 6.0
    values = np.exp(-offsets * offsets / (2.0 * spread * spread))
    return values / values.sum()


def filter_table(cells, first_taps, second_taps, guard, order):
    out_count = cells // 4
    shape = tuple(((cells + 10, 2, out_count)[d] for d in order))
    where = {d: order.index(d) for d in range(3)}
    position = lax.broadcasted_iota(jnp.int32, shape, where[0])
    which = lax.broadcasted_iota(jnp.int32, shape, where[1])
    out_index = lax.broadcasted_iota(jnp.int32, shape, where[2])
    tap_at = position - 1 - 4 * out_index + guard
    table = jnp.zeros(shape, jnp.float32)
    for tap_index in range(13):
        value = jnp.where(
            which == 0, np.float32(first_taps[tap_index]), np.float32(second_taps[tap_index])
        )
        table = jnp.where(tap_at == tap_index, value, table)
    return table


def library(narrow_part, broad_part):
    product = (
        narrow_part.astype(jnp.float32)[:, None, :] * broad_part.astype(jnp.float32)[None, :, :]
    )
    return product.astype(jnp.bfloat16).reshape(
        narrow_part.shape[0] * broad_part.shape[0], narrow_part.shape[1]
    )


def local(fields, stresses, planes, active_masks):
    chan_dev, plane_count, cells_x, cells_z = fields.shape
    coarse_x = cells_x // 4
    coarse_z = cells_z // 4
    row_count = plane_count * coarse_x * coarse_z
    col_devices = lax.axis_size("cols")
    column_index = lax.axis_index("cols")
    term_dev = TERMS // col_devices
    offset = column_index * term_dev
    samples = float(row_count * lax.axis_size("slab") * lax.axis_size("rep"))
    height = 2.0 * (planes.astype(jnp.float32) + 0.5) / NY - 1.0
    root_weight = jnp.sqrt(1.2 - height * height)
    padded = extended(fields, (("slab", 3), ("rep", 2)), 5)
    widened = padded.astype(jnp.float32)
    narrow_taps = kernel(1.5)
    broad_taps = kernel(3.0)
    guard = jnp.minimum(lax.axis_index("rep"), 0)
    span_table = filter_table(cells_z, narrow_taps, broad_taps, guard, (0, 1, 2))
    stream_table = filter_table(cells_x, narrow_taps, broad_taps, guard, (1, 0, 2))
    along_span = jnp.einsum("cpxz,zsn->cpxsn", widened, span_table, precision=lax.Precision.HIGHEST)
    filtered = jnp.einsum(
        "cpxsn,sxm->scpmn", along_span, stream_table, precision=lax.Precision.HIGHEST
    )
    narrow = filtered[0]
    broader = filtered[1]
    narrow_set = narrow.astype(jnp.bfloat16).reshape(chan_dev, row_count)
    broad_set = (
        (broader * root_weight[None, :, None, None])
        .astype(jnp.bfloat16)
        .reshape(chan_dev, row_count)
    )
    weighted = (stresses.astype(jnp.float32) * root_weight[None, :, None, None]).astype(
        jnp.bfloat16
    )
    weighted = weighted.reshape(STRESS, row_count)
    chunk = row_count // col_devices
    block_rows = math.gcd(chunk, 4096)
    block_count = chunk // block_rows
    both_sets = lax.all_to_all(jnp.stack([narrow_set, broad_set]), "cols", 2, 1, tiled=True)
    narrow_all, broad_all = (both_sets[0], both_sets[1])
    weighted = lax.dynamic_slice_in_dim(weighted, column_index * chunk, chunk, 1)

    def gram_step(block_index, carry):
        gram_acc, rhs_acc = carry
        start = block_index * block_rows
        narrow_piece = lax.dynamic_slice_in_dim(narrow_all, start, block_rows, 1)
        broad_piece = lax.dynamic_slice_in_dim(broad_all, start, block_rows, 1)
        all_terms = library(narrow_piece, broad_piece)
        weighted_piece = lax.dynamic_slice_in_dim(weighted, start, block_rows, 1)
        gram_acc = gram_acc + jnp.einsum(
            "ir,jr->ij", all_terms, all_terms, preferred_element_type=jnp.float32
        )
        rhs_acc = rhs_acc + jnp.einsum(
            "ir,kr->ik", all_terms, weighted_piece, preferred_element_type=jnp.float32
        )
        return (gram_acc, rhs_acc)

    gram_part, rhs_part = lax.fori_loop(
        0,
        block_count,
        gram_step,
        (jnp.zeros((TERMS, TERMS), jnp.float32), jnp.zeros((TERMS, STRESS), jnp.float32)),
    )
    full_rows = tree_sum(jnp.concatenate([gram_part, rhs_part], axis=1), ("rep", "slab", "cols"))
    gram_matrix = full_rows[:, :TERMS]
    rhs_sums = full_rows[:, TERMS:]
    column_scale = 1.0 / jnp.sqrt(jnp.diagonal(gram_matrix) / samples + epsilon)
    normal_gram = column_scale[:, None] * gram_matrix * column_scale[None, :] / samples
    target_norm = column_scale[None, :] * rhs_sums.T / samples

    def apply_normal(vector, active):
        product = jnp.einsum(
            "kl,il->ki", active * vector, normal_gram, precision=lax.Precision.HIGHEST
        )
        return active * product + ridge_weight * vector

    def cg_turn(turn_index, state):
        solution_all, remain, direction, norm_now, active = state
        applied = apply_normal(direction, active)
        curve_sum = jnp.sum(direction * applied, axis=1)
        step_size = norm_now / (curve_sum + epsilon)
        solution_all = solution_all + step_size[:, None] * direction
        remain = remain - step_size[:, None] * applied
        norm_next = jnp.sum(remain * remain, axis=1)
        direction = remain + (norm_next / (norm_now + epsilon))[:, None] * direction
        return (solution_all, remain, direction, norm_next, active)

    def cg_pass(pass_index, state):
        solution_all, coefficients = state
        active = lax.dynamic_index_in_dim(active_masks, pass_index, 0, keepdims=False)
        active = active.astype(jnp.float32)
        solution_all = active * solution_all
        remain = active * target_norm - apply_normal(solution_all, active)
        norm_now = jnp.sum(remain * remain, axis=1)
        solution_all = lax.fori_loop(
            0, ITERS, cg_turn, (solution_all, remain, remain, norm_now, active)
        )[0]
        own_part = lax.dynamic_slice_in_dim(solution_all, offset, term_dev, 1)
        coefficients = lax.dynamic_update_index_in_dim(coefficients, own_part, pass_index, 0)
        return (solution_all, coefficients)

    solution_all, coefficients = lax.fori_loop(
        0,
        PASSES,
        cg_pass,
        (
            jnp.zeros((STRESS, TERMS), jnp.float32),
            jnp.zeros((PASSES, STRESS, term_dev), jnp.float32),
        ),
    )
    final_weights = (column_scale[None, :] * solution_all).astype(jnp.bfloat16)

    def misfit_step(block_index, misfit_acc):
        start = block_index * block_rows
        narrow_piece = lax.dynamic_slice_in_dim(narrow_all, start, block_rows, 1)
        broad_piece = lax.dynamic_slice_in_dim(broad_all, start, block_rows, 1)
        all_terms = library(narrow_piece, broad_piece)
        predicted = jnp.dot(final_weights, all_terms, preferred_element_type=jnp.float32)
        weighted_piece = lax.dynamic_slice_in_dim(weighted, start, block_rows, 1)
        piece_misfit = (weighted_piece.astype(jnp.float32) - predicted).astype(jnp.bfloat16)
        return lax.dynamic_update_slice_in_dim(misfit_acc, piece_misfit, start, 1)

    misfit = lax.fori_loop(0, block_count, misfit_step, jnp.zeros((STRESS, chunk), jnp.bfloat16))
    misfit = lax.all_gather(misfit, "cols", axis=1, tiled=True)
    misfit = misfit.reshape(STRESS, plane_count, coarse_x, coarse_z)
    return (coefficients, misfit)


def solution(mesh):
    placed = (
        P("cols", "groups", "rep", "slab"),
        P(None, "groups", "rep", "slab"),
        P("groups"),
        P(),
    )
    return jax.shard_map(
        local,
        mesh=mesh,
        in_specs=placed,
        out_specs=(P(None, "groups", "cols"), P(None, "groups", "rep", "slab")),
        check_vma=False,
    )
```

profile of v0, /device:TPU:0, one launch (start us, length us, event | category | flops | bytes accessed | tf_op | source)
XLA Modules:
  0.0 642.4 jit_solution(13972069590268491912)
XLA Ops:
  0.7 11.6 %copy.29 = bf16[4,4,1024,256]{2,3,1,0:T(8,128)(2,1)} copy(bf16[4,4,1024,256]{3,2,1,0:T(8,128)(2,1)} %param.12) | data formatting | bytes 16777216 | tf_op args[0]
  12.2 1.1 fusion.185
  13.4 3.0 collective-permute-start
  16.9 6.6 %collective-permute-done = bf16[4,4,1024,5]{2,3,1,0:T(8,128)(2,1)S(1)} collective-permute-done((bf16[4,4,1024,5]{2,3,1,0:T(8,128)(2,1)S(1)}, bf16[4,4,1024,5]{2,3,1,0:T(8,128)(2,1)S(1)}, u32[]{:S(2)}, u32[]{:S(2)}) %collective-permute-start) | collective-permute-done | bytes 163872 | tf_op jit(solution)/shard_map/ppermute | solution.py:24
  23.5 4.8 collective-permute-done.1
  28.3 5.5 pad_maximum_fusion
  33.8 3.5 copy-done
  40.6 0.8 copy.41
  41.5 2.3 reshape.115
  45.0 18.4 %concatenate.14 = bf16[4,4,1034,266]{2,3,1,0:T(8,128)(2,1)} concatenate(bf16[4,4,5,266]{2,3,1,0:T(8,128)(2,1)S(1)} %copy.34, bf16[4,4,1024,266]{2,3,1,0:T(8,128)(2,1)} %copy-done, bf16[4,4,5,266]{2,3,1,0:T(8,128)(2,1)S(1)} %copy.35), dimensions={2} | concatenate | bytes 17602816 | tf_op jit(solution)/shard_map/concatenate | solution.py:26
  63.4 10.7 %fusion.10 = f32[4,4,1034,2,64]{2,4,1,0,3:T(8,128)S(1)} fusion(bf16[4,4,1034,266]{2,3,1,0:T(8,128)(2,1)} %concatenate.14, f32[2]{0:T(128)S(1)} %get-tuple-element.567, f32[2]{0:T(128)S(1)} %get-tuple-element.568, f32[2]{0:T(128)S(1)} %get-tuple-element.569, f32[2]{0:T(128)S(1)} %get-tuple-element.570, f32[2]{0:T(128)S(1)} %get-tuple-element.571, ...), kind=kOutput, calls=%fused_computation.32 | convolution fusion | flops 6760434688 | bytes 17273316 | tf_op jit(solution)/shard_map/cpxz,zsn->cpxsn/dot_general | solution.py:95
  74.2 10.1 %fusion.53 = f32[2,4,4,256,64]{3,4,2,1,0:T(8,128)S(1)} fusion(f32[4,4,1034,2,64]{2,4,1,0,3:T(8,128)S(1)} %fusion.10, f32[2]{0:T(128)S(1)} %get-tuple-element.567, f32[2]{0:T(128)S(1)} %get-tuple-element.568, f32[2]{0:T(128)S(1)} %get-tuple-element.569, f32[2]{0:T(128)S(1)} %get-tuple-element.570, f32[2]{0:T(128)S(1)} %get-tuple-element.571, ...), kind=kOutput, calls=%fused_computation.64 | convolution fusion | flops 6520188928 | bytes 10572900 | tf_op jit(solution)/shard_map/cpxsn,sxm->scpmn/dot_general | solution.py:96
  84.4 0.9 slice.62
  85.9 0.9 squeeze.18
  86.7 1.5 copy.36
  88.9 1.2 multiply_convert_fusion.3
  90.9 50.9 %copy.38 = bf16[2,4,65536]{1,0,2:T(2,128)(2,1)} copy(bf16[2,4,65536]{2,1,0:T(4,128)(2,1)S(1)} %pad_maximum_fusion.1) | data formatting | bytes 2097152 | tf_op jit(solution)/shard_map/stack | solution.py:114
  141.8 99.7 %reshape.126 = bf16[4,2,65536]{2,1,0:T(2,128)(2,1)} reshape(bf16[65536,2,4]{2,1,0:T(2,128)(2,1)} %bitcast.80) | data formatting | bytes 2097152
  241.5 5.1 all-to-all-start
  246.6 1.7 constant_dynamic-slice_fusion
  248.3 24.3 %all-to-all-done = bf16[4,2,65536]{2,1,0:T(2,128)(2,1)S(1)} async-done(((bf16[4,2,65536]{2,1,0:T(2,128)(2,1)}), bf16[4,2,65536]{2,1,0:T(2,128)(2,1)S(1)}, u32[]{:S(2)}, u32[]{:S(2)}) %all-to-all-start) | async-done | bytes 1048608 | tf_op jit(solution)/shard_map/all_to_all | solution.py:114
  272.6 85.1 %reshape.127 = bf16[65536,2,4]{2,1,0:T(2,128)(2,1)} reshape(bf16[4,2,65536]{2,1,0:T(2,128)(2,1)S(1)} %all-to-all-done) | data formatting | bytes 2097152
  357.7 62.4 %fusion.183 = (bf16[1,4,4,16384]{2,0,3,1:T(2,128)(2,1)}, bf16[1,4,4,16384]{2,0,3,1:T(2,128)(2,1)}) fusion(bf16[2,4,4,16384]{2,0,3,1:T(2,128)(2,1)} %bitcast.78), kind=kLoop, calls=%fused_computation.197 | loop fusion | bytes 2097152 | tf_op jit(solution)/shard_map/slice | solution.py:115
  420.1 61.1 %copy.39 = bf16[1,4,4,16384]{3,2,1,0:T(4,128)(2,1)S(1)} copy(bf16[1,4,4,16384]{2,0,3,1:T(2,128)(2,1)} %get-tuple-element.562) | data formatting | bytes 1048576 | tf_op jit(solution)/shard_map/slice | solution.py:115
  481.3 61.1 %copy.40 = bf16[1,4,4,16384]{3,2,1,0:T(4,128)(2,1)S(1)} copy(bf16[1,4,4,16384]{2,0,3,1:T(2,128)(2,1)} %get-tuple-element.561) | data formatting | bytes 1048576 | tf_op jit(solution)/shard_map/slice | solution.py:115
  542.5 11.0 %while.79 = (s32[]{:T(128)}, f32[256,256]{1,0:T(8,128)S(1)}, f32[256,6]{0,1:T(8,128)S(1)}, bf16[16,16384]{1,0:T(8,128)(2,1)S(1)}, bf16[16,16384]{1,0:T(8,128)(2,...) while((s32[]{:T(128)}, f32[256,256]{1,0:T(8,128)S(1)}, ...), condition=%wide.region_1.2_spmd.clone, body=%wide.region_0.1_spmd.clone.sunk | while | flops 551816192 | bytes 8204454 | solution.py:133
  544.0 1.5 convolution_add_fusion.5
  546.7 1.5 convolution_add_fusion.5
  549.3 1.5 convolution_add_fusion.5
  552.0 1.5 convolution_add_fusion.5
  553.8 1.7 collective-permute-done.4
  555.5 1.6 collective-permute-start.5
  557.1 9.7 %collective-permute-done.5 = f32[256,262]{1,0:T(8,128)S(1)} collective-permute-done((f32[256,262]{1,0:T(8,128)S(1)}, f32[256,262]{1,0:T(8,128)S(1)}, u32[]{:S(2)}, u32[]{:S(2)}) %collective-permute-start.5) | collective-permute-done | bytes 268320 | tf_op jit(solution)/shard_map/ppermute | solution.py:39
  566.9 10.3 %collective-permute-done.6 = f32[256,262]{1,0:T(8,128)S(1)} collective-permute-done((f32[256,262]{1,0:T(8,128)S(1)}, f32[256,262]{1,0:T(8,128)S(1)}, u32[]{:S(2)}, u32[]{:S(2)}) %collective-permute-start.6) | collective-permute-done | bytes 268320 | tf_op jit(solution)/shard_map/ppermute | solution.py:39
  577.6 18.5 %collective-permute-done.7 = f32[256,262]{1,0:T(8,128)S(1)} collective-permute-done((f32[256,262]{1,0:T(8,128)S(1)}, f32[256,262]{1,0:T(8,128)S(1)}, u32[]{:S(2)}, u32[]{:S(2)}) %collective-permute-start.7) | collective-permute-done | bytes 268320 | tf_op jit(solution)/shard_map/ppermute | solution.py:39
  596.1 2.3 gather_fusion
  598.8 12.1 %while.77 = (s32[]{:T(128)}, f32[6,256]{1,0:T(8,128)S(1)}, f32[3,6,64]{2,1,0:T(8,128)}, s32[3,6,256]{2,1,0:T(8,128)}, f32[6,256]{1,0:T(8,128)S(1)}, /*index=5*/f...) while((s32[]{:T(128)}, f32[6,256]{1,0:T(8,128)S(1)}, f32[3,6,64]{2,1,0:T(8,128)}, ...), condition=%wide.region_8.9_spmd, body=%wide.region_2.8_spmd.sunk | while | flops 9474058 | bytes 660566 | solution.py:177
  599.9 2.2 while.80
  604.0 2.2 while.80
  608.0 2.2 while.80
  610.9 6.4 %while.78 = (s32[]{:T(128)}, bf16[6,16384]{1,0:T(8,128)(2,1)S(1)}, bf16[6,16384]{1,0:T(8,128)(2,1)}, bf16[16,16384]{1,0:T(8,128)(2,1)S(1)}, bf16[16,16384]{1,0:T...) while((s32[]{:T(128)}, bf16[6,16384]{1,0:T(8,128)(2,1)S(1)}, ...), condition=%wide.region_10.11_spmd, body=%wide.region_9.10_spmd.sunk | while | flops 14884870 | bytes 5623963 | solution.py:198
  611.3 1.2 fusion.208
  612.9 1.2 fusion.208
  614.5 1.2 fusion.208
  616.1 1.2 fusion.208
  617.4 21.5 %all_gather.3 = bf16[6,65536]{1,0:T(8,128)(2,1)S(1)} all-gather(bf16[6,16384]{1,0:T(8,128)(2,1)S(1)} %get-tuple-element.439), channel_id=1, replica_groups=mesh['groups'=2,'cols'=4,'slab'=2,'rep'=2] {'cols'}, dimensions={1}, use_global_device_ids=true | all-gather | bytes 983040 | tf_op jit(solution)/shard_map/all_gather | solution.py:199
  638.9 1.6 reshape.116
  640.5 1.4 copy.44
  (140 shorter events, 26.6 us)
Async XLA Ops:
  0.6 15.8 %copy-start.2 = (s32[4]{0:T(128)S(1)}, s32[4]{0:T(128)}, u32[]{:S(2)}) copy-start(s32[4]{0:T(128)} %param.14) | copy-start | bytes 52
  0.6 15.9 %copy-start.1 = (bf16[6,4,256,64]{2,3,1,0:T(8,128)(2,1)S(1)}, bf16[6,4,256,64]{2,3,1,0:T(8,128)(2,1)}, u32[]{:S(2)}) copy-start(bf16[6,4,256,64]{2,3,1,0:T(8,128)(2,1)} %param.13) | copy-start | bytes 2359300
  13.4 10.1 %collective-permute-start = (bf16[4,4,1024,5]{2,3,1,0:T(8,128)(2,1)S(1)}, bf16[4,4,1024,5]{2,3,1,0:T(8,128)(2,1)S(1)}, u32[]{:S(2)}, u32[]{:S(2)}) collective-permute-start(bf16[4,4,1024,5]{2,3,1,0:T(8,128)(2,1)S(1)} %get-tuple-element.565), channel_id=1, source_target_pairs={{0,2},{2,0},{1,3},{3,1},{4,6},{6,4},{5,7},{7,5},{8,10},{10,8},{9,1... | collective-permute-start | bytes 491528 | tf_op jit(solution)/shard_map/ppermute | solution.py:24
  16.4 11.9 %collective-permute-start.1 = (bf16[4,4,1024,5]{2,3,1,0:T(8,128)(2,1)S(1)}, bf16[4,4,1024,5]{2,3,1,0:T(8,128)(2,1)S(1)}, u32[]{:S(2)}, u32[]{:S(2)}) collective-permute-start(bf16[4,4,1024,5]{2,3,1,0:T(8,128)(2,1)S(1)} %get-tuple-element.566), channel_id=1, source_target_pairs={{2,0},{0,2},{3,1},{1,3},{6,4},{4,6},{7,5},{5,7},{10,8},{8,10},{11,... | collective-permute-start | bytes 491528 | tf_op jit(solution)/shard_map/ppermute | solution.py:25
  33.8 3.5 copy-start
  38.5 5.3 collective-permute-start.2
  39.1 5.3 collective-permute-start.3
  241.5 31.1 %all-to-all-start = ((bf16[4,2,65536]{2,1,0:T(2,128)(2,1)}), bf16[4,2,65536]{2,1,0:T(2,128)(2,1)S(1)}, u32[]{:S(2)}, u32[]{:S(2)}) async-start(bf16[4,2,65536]{2,1,0:T(2,128)(2,1)} %reshape.126), calls=%async_computation | async-start | bytes 2097152 | tf_op jit(solution)/shard_map/all_to_all | solution.py:114
  553.7 1.8 collective-permute-start.4
  555.5 11.2 %collective-permute-start.5 = (f32[256,262]{1,0:T(8,128)S(1)}, f32[256,262]{1,0:T(8,128)S(1)}, u32[]{:S(2)}, u32[]{:S(2)}) collective-permute-start(f32[256,262]{1,0:T(8,128)S(1)} %fusion.181), channel_id=1, source_target_pairs={{0,2},{2,0},{1,3},{3,1},{4,6},{6,4},{5,7},{7,5},{8,10},{10,8},{9,1... | collective-permute-start | bytes 804872 | tf_op jit(solution)/shard_map/ppermute | solution.py:39
  566.8 10.4 %collective-permute-start.6 = (f32[256,262]{1,0:T(8,128)S(1)}, f32[256,262]{1,0:T(8,128)S(1)}, u32[]{:S(2)}, u32[]{:S(2)}) collective-permute-start(f32[256,262]{1,0:T(8,128)S(1)} %add.190), channel_id=1, source_target_pairs={{0,4},{4,0},{8,12},{12,8},{1,5},{5,1},{9,13},{13,9},{2,6},{6,2},{1... | collective-permute-start | bytes 804872 | tf_op jit(solution)/shard_map/ppermute | solution.py:39
  577.2 18.8 %collective-permute-start.7 = (f32[256,262]{1,0:T(8,128)S(1)}, f32[256,262]{1,0:T(8,128)S(1)}, u32[]{:S(2)}, u32[]{:S(2)}) collective-permute-start(f32[256,262]{1,0:T(8,128)S(1)} %add.191), channel_id=1, source_target_pairs={{0,8},{4,12},{8,0},{12,4},{1,9},{5,13},{9,1},{13,5},{2,10},{6,14},... | collective-permute-start | bytes 804872 | tf_op jit(solution)/shard_map/ppermute | solution.py:39
where the time goes:
time: 654 us; the launch traced here: 642 us
  local copies, waits for them, and re-layouts  476 us (73%)
  waiting for transfers between devices  75.8 us (12%)
  matrix products  40.1 us (6%)
  blocking collectives  21.5 us (3%)
  other arithmetic  15.8 us (2%)
  starting transfers between devices  10.9 us (2%)
    unnamed x10, local copies, waits for them, and re-layouts  201 us
    slice x3, local copies, waits for them, and re-layouts, local(): narrow_all, broad_all = (both_sets[0], both_sets[1])  185 us
    another operation x1, local copies, waits for them, and re-layouts, local(): jnp.stack([narrow_set, broad_set])  50.9 us
    ppermute x4, waiting for transfers between devices, tree_sum(): value = value + lax.ppermute(value, axis, partner)  40.1 us
    all_to_all x1, waiting for transfers between devices, local(): lax.all_to_all(jnp.stack([narrow_set, broad_set]), 'cols', 2, 1, tiled=True)  24.3 us
    all_gather x1, blocking collectives, local(): misfit = lax.all_gather(misfit, 'cols', axis=1, tiled=True)  21.5 us
    concatenate x1, local copies, waits for them, and re-layouts, extended(): array = jnp.concatenate([before, array, after], axis=dim)  18.4 us
  transfers between devices with their start and end apart: 9, of which 7 were waited for; matrix products, arithmetic and copies ran while one was open for 1% of the time, Pallas kernels for 0%

commit v1 on v0

--- a/solution.py
+++ b/solution.py
@@ -111,7 +111,20 @@
     chunk = row_count // col_devices
     block_rows = math.gcd(chunk, 4096)
     block_count = chunk // block_rows
-    both_sets = lax.all_to_all(jnp.stack([narrow_set, broad_set]), "cols", 2, 1, tiled=True)
+    shard = jnp.stack([narrow_set, broad_set])
+    ways, here = (lax.axis_size("cols"), lax.axis_index("cols"))
+    width_2 = shard.shape[2] // ways
+    dims = list(shard.shape)
+    dims[2] = width_2
+    height_2 = dims[1]
+    dims[1] = height_2 * ways
+    full = jnp.zeros(dims, shard.dtype)
+    for mask in range(ways):
+        part = lax.dynamic_slice_in_dim(shard, (here ^ mask) * width_2, width_2, axis=2)
+        if mask:
+            part = lax.ppermute(part, "cols", [(d_2, d_2 ^ mask) for d_2 in range(ways)])
+        full = lax.dynamic_update_slice_in_dim(full, part, (here ^ mask) * height_2, axis=1)
+    both_sets = full
     narrow_all, broad_all = (both_sets[0], both_sets[1])
     weighted = lax.dynamic_slice_in_dim(weighted, column_index * chunk, chunk, 1)
 

time: 654 us -> 219 us (0.33); the launches traced: 642 us -> 217 us
  local copies, waits for them, and re-layouts: 476 us -> 55.6 us
  waiting for transfers between devices: 75.8 us -> 66.2 us
  starting transfers between devices: 10.9 us -> 17.5 us
    unnamed x10 -> x8, local copies, waits for them, and re-layouts: 201 us -> 16.5 us
    slice x3 -> x0, local copies, waits for them, and re-layouts: 185 us -> none  [local(): narrow_all, broad_all = (both_sets[0], both_sets[1])]
    another operation x1 -> x0, local copies, waits for them, and re-layouts: 50.9 us -> none  [local(): jnp.stack([narrow_set, broad_set])]
    all_to_all x1 -> x0, waiting for transfers between devices: 24.3 us -> none  [local(): lax.all_to_all(jnp.stack([narrow_set, broad_set]), 'cols', 2, 1, tiled=True)]
    ppermute x0 -> x3, waiting for transfers between devices: none -> 18.6 us  [local(): lax.ppermute(part, 'cols', [(d_2, d_2 ^ mask) for d_2 in range(ways)])]
    ppermute x4, starting transfers between devices: 2.04 us -> 9.32 us  [tree_sum(): value = value + lax.ppermute(value, axis, partner)]
  transfers between devices with their start and end apart: 9 -> 11, of which waited for: 7 -> 8; matrix products, arithmetic and copies ran while one was open for 1% -> 3% of each run, Pallas kernels for 0% -> 0%
where the time goes in v1:
time: 219 us; the launch traced here: 217 us
  waiting for transfers between devices  66.2 us (30%)
  local copies, waits for them, and re-layouts  55.6 us (25%)
  matrix products  40 us (18%)
  blocking collectives  21.7 us (10%)
  starting transfers between devices  17.5 us (8%)
  other arithmetic  15 us (7%)
    ppermute x4, waiting for transfers between devices, tree_sum(): value = value + lax.ppermute(value, axis, partner)  36.2 us
    all_gather x1, blocking collectives, local(): misfit = lax.all_gather(misfit, 'cols', axis=1, tiled=True)  21.7 us
    ppermute x3, waiting for transfers between devices, local(): lax.ppermute(part, 'cols', [(d_2, d_2 ^ mask) for d_2 in range(ways)])  18.6 us
    concatenate x1, local copies, waits for them, and re-layouts, extended(): array = jnp.concatenate([before, array, after], axis=dim)  18.4 us
    unnamed x8, local copies, waits for them, and re-layouts  16.5 us
    dot_general x1, matrix products, local(): jnp.einsum('cpxz,zsn->cpxsn', widened, span_table, precision=lax.Precisio...  10.7 us
    dot_general x1, matrix products, local(): jnp.einsum('cpxsn,sxm->scpmn', along_span, stream_table, precision=lax.Pr...  10.1 us
    ppermute x4, starting transfers between devices, tree_sum(): value = value + lax.ppermute(value, axis, partner)  9.32 us
  transfers between devices with their start and end apart: 11, of which 8 were waited for; matrix products, arithmetic and copies ran while one was open for 3% of the time, Pallas kernels for 0%

profile of v1, /device:TPU:0, one launch (start us, length us, event | category | flops | bytes accessed | tf_op | source)
XLA Modules:
  0.0 217.4 jit_solution(6348570329536142480)
XLA Ops:
  0.7 11.6 %copy.24 = bf16[4,4,1024,256]{2,3,1,0:T(8,128)(2,1)} copy(bf16[4,4,1024,256]{3,2,1,0:T(8,128)(2,1)} %param.12) | data formatting | bytes 16777216 | tf_op args[0]
  12.2 1.1 fusion.189
  13.4 3.0 %collective-permute-start = (bf16[4,4,1024,5]{2,3,1,0:T(8,128)(2,1)S(1)}, bf16[4,4,1024,5]{2,3,1,0:T(8,128)(2,1)S(1)}, u32[]{:S(2)}, u32[]{:S(2)}) collective-permute-start(bf16[4,4,1024,5]{2,3,1,0:T(8,128)(2,1)S(1)} %get-tuple-element.563), channel_id=1, source_target_pairs={{0,2},{2,0},{1,3},{3,1},{4,6},{6,4},{5,7},{7,5},{8,10},{10,8},{9,1... | collective-permute-start | bytes 491528 | tf_op jit(solution)/shard_map/ppermute | solution.py:24
  16.9 6.6 %collective-permute-done = bf16[4,4,1024,5]{2,3,1,0:T(8,128)(2,1)S(1)} collective-permute-done((bf16[4,4,1024,5]{2,3,1,0:T(8,128)(2,1)S(1)}, bf16[4,4,1024,5]{2,3,1,0:T(8,128)(2,1)S(1)}, u32[]{:S(2)}, u32[]{:S(2)}) %collective-permute-start) | collective-permute-done | bytes 163872 | tf_op jit(solution)/shard_map/ppermute | solution.py:24
  23.5 4.8 %collective-permute-done.1 = bf16[4,4,1024,5]{2,3,1,0:T(8,128)(2,1)S(1)} collective-permute-done((bf16[4,4,1024,5]{2,3,1,0:T(8,128)(2,1)S(1)}, bf16[4,4,1024,5]{2,3,1,0:T(8,128)(2,1)S(1)}, u32[]{:S(2)}, u32[]{:S(2)}) %collective-permute-start.1) | collective-permute-done | bytes 163872 | tf_op jit(solution)/shard_map/ppermute | solution.py:25
  28.3 5.5 %pad_maximum_fusion = bf16[4,4,1024,266]{2,3,1,0:T(8,128)(2,1)S(1)} fusion(bf16[4,4,1024,5]{2,3,1,0:T(8,128)(2,1)S(1)} %collective-permute-done.1, bf16[4,4,1024,256]{2,3,1,0:T(8,128)(2,1)} %copy.24, bf16[4,4,1024,5]{2,3,1,0:T(8,128)(2,1)S(1)} %collective-permute-done), kind=kLoop, calls=%fused_computation.34 | loop fusion | flops 26148864 | bytes 17432576 | tf_op jit(solution)/shard_map/concatenate | solution.py:26
  33.8 3.5 %copy-done = bf16[4,4,1024,266]{2,3,1,0:T(8,128)(2,1)} copy-done((bf16[4,4,1024,266]{2,3,1,0:T(8,128)(2,1)}, bf16[4,4,1024,266]{2,3,1,0:T(8,128)(2,1)S(1)}, u32[]{:S(2)}) %copy-start) | copy-done | bytes 8716312
  39.9 0.9 copy.33
  40.8 2.3 %reshape.111 = bf16[6,65536]{1,0:T(8,128)(2,1)} reshape(bf16[6,4,256,64]{3,2,1,0:T(8,128)(2,1)S(1)} %copy.33) | data formatting | bytes 1572864 | tf_op jit(solution)/shard_map/reshape | solution.py:110
  44.3 18.4 %concatenate.14 = bf16[4,4,1034,266]{2,3,1,0:T(8,128)(2,1)} concatenate(bf16[4,4,5,266]{2,3,1,0:T(8,128)(2,1)S(1)} %copy.29, bf16[4,4,1024,266]{2,3,1,0:T(8,128)(2,1)} %copy-done, bf16[4,4,5,266]{2,3,1,0:T(8,128)(2,1)S(1)} %copy.30), dimensions={2} | concatenate | bytes 17602816 | tf_op jit(solution)/shard_map/concatenate | solution.py:26
  62.7 10.7 %fusion.10 = f32[4,4,1034,2,64]{2,4,1,0,3:T(8,128)S(1)} fusion(bf16[4,4,1034,266]{2,3,1,0:T(8,128)(2,1)} %concatenate.14, f32[2]{0:T(128)S(1)} %get-tuple-element.571, f32[2]{0:T(128)S(1)} %get-tuple-element.572, f32[2]{0:T(128)S(1)} %get-tuple-element.573, f32[2]{0:T(128)S(1)} %get-tuple-element.574, f32[2]{0:T(128)S(1)} %get-tuple-element.575, ...), kind=kOutput, calls=%fused_computation.32 | convolution fusion | flops 6760434688 | bytes 17273316 | tf_op jit(solution)/shard_map/cpxz,zsn->cpxsn/dot_general | solution.py:95
  73.4 10.1 %fusion.53 = f32[2,4,4,256,64]{3,4,2,1,0:T(8,128)S(1)} fusion(f32[4,4,1034,2,64]{2,4,1,0,3:T(8,128)S(1)} %fusion.10, f32[2]{0:T(128)S(1)} %get-tuple-element.571, f32[2]{0:T(128)S(1)} %get-tuple-element.572, f32[2]{0:T(128)S(1)} %get-tuple-element.573, f32[2]{0:T(128)S(1)} %get-tuple-element.574, f32[2]{0:T(128)S(1)} %get-tuple-element.575, ...), kind=kOutput, calls=%fused_computation.64 | convolution fusion | flops 6520188928 | bytes 10572900 | tf_op jit(solution)/shard_map/cpxsn,sxm->scpmn/dot_general | solution.py:96
  83.6 0.9 slice.62
  85.1 0.9 squeeze.18
  85.9 1.5 copy.31
  88.5 0.9 fusion.80
  89.4 1.9 collective-permute-start.4
  91.3 1.7 constant_dynamic-slice_fusion
  92.9 2.6 %collective-permute-start.5 = (bf16[2,4,16384]{2,1,0:T(4,128)(2,1)S(1)}, bf16[2,4,16384]{2,1,0:T(4,128)(2,1)S(1)}, u32[]{:S(2)}, u32[]{:S(2)}) collective-permute-start(bf16[2,4,16384]{2,1,0:T(4,128)(2,1)S(1)} %get-tuple-element.570), channel_id=1, source_target_pairs={{0,8},{4,12},{8,0},{12,4},{1,9},{5,13},{9,1},{13,5},{2,10},{6,14},... | collective-permute-start | bytes 786440 | tf_op jit(solution)/shard_map/ppermute | solution.py:125
  95.5 6.1 %collective-permute-done.4 = bf16[2,4,16384]{2,1,0:T(4,128)(2,1)S(1)} collective-permute-done((bf16[2,4,16384]{2,1,0:T(4,128)(2,1)S(1)}, bf16[2,4,16384]{2,1,0:T(4,128)(2,1)S(1)}, u32[]{:S(2)}, u32[]{:S(2)}) %collective-permute-start.4) | collective-permute-done | bytes 262176 | tf_op jit(solution)/shard_map/ppermute | solution.py:125
  101.8 12.5 %collective-permute-done.5 = bf16[2,4,16384]{2,1,0:T(4,128)(2,1)S(1)} collective-permute-done((bf16[2,4,16384]{2,1,0:T(4,128)(2,1)S(1)}, bf16[2,4,16384]{2,1,0:T(4,128)(2,1)S(1)}, u32[]{:S(2)}, u32[]{:S(2)}) %collective-permute-start.5) | collective-permute-done | bytes 262176 | tf_op jit(solution)/shard_map/ppermute | solution.py:125
  114.8 10.7 %while.79 = (s32[]{:T(128)}, f32[256,256]{1,0:T(8,128)S(1)}, f32[256,6]{0,1:T(8,128)S(1)}, bf16[16,16384]{1,0:T(8,128)(2,1)S(1)}, bf16[16,16384]{1,0:T(8,128)(2,...) while((s32[]{:T(128)}, f32[256,256]{1,0:T(8,128)S(1)}, ...), condition=%wide.region_1.2_spmd.clone, body=%wide.region_0.1_spmd.clone.sunk | while | flops 551816192 | bytes 8204454 | solution.py:146
  115.2 0.8 convolution_add_fusion.4
  116.0 1.5 convolution_add_fusion.5
  118.6 1.5 convolution_add_fusion.5
  120.5 0.8 convolution_add_fusion.4
  121.3 1.5 convolution_add_fusion.5
  124.0 1.5 convolution_add_fusion.5
  125.7 1.7 collective-permute-done.7
  127.5 1.6 collective-permute-start.8
  129.1 9.7 %collective-permute-done.8 = f32[256,262]{1,0:T(8,128)S(1)} collective-permute-done((f32[256,262]{1,0:T(8,128)S(1)}, f32[256,262]{1,0:T(8,128)S(1)}, u32[]{:S(2)}, u32[]{:S(2)}) %collective-permute-start.8) | collective-permute-done | bytes 268320 | tf_op jit(solution)/shard_map/ppermute | solution.py:39
  138.8 4.8 %collective-permute-start.9 = (f32[256,262]{1,0:T(8,128)S(1)}, f32[256,262]{1,0:T(8,128)S(1)}, u32[]{:S(2)}, u32[]{:S(2)}) collective-permute-start(f32[256,262]{1,0:T(8,128)S(1)} %add.219), channel_id=1, source_target_pairs={{0,4},{4,0},{8,12},{12,8},{1,5},{5,1},{9,13},{13,9},{2,6},{6,2},{1... | collective-permute-start | bytes 804872 | tf_op jit(solution)/shard_map/ppermute | solution.py:39
  143.6 8.6 %collective-permute-done.9 = f32[256,262]{1,0:T(8,128)S(1)} collective-permute-done((f32[256,262]{1,0:T(8,128)S(1)}, f32[256,262]{1,0:T(8,128)S(1)}, u32[]{:S(2)}, u32[]{:S(2)}) %collective-permute-start.9) | collective-permute-done | bytes 268320 | tf_op jit(solution)/shard_map/ppermute | solution.py:39
  152.2 2.8 %collective-permute-start.10 = (f32[256,262]{1,0:T(8,128)S(1)}, f32[256,262]{1,0:T(8,128)S(1)}, u32[]{:S(2)}, u32[]{:S(2)}) collective-permute-start(f32[256,262]{1,0:T(8,128)S(1)} %add.220), channel_id=1, source_target_pairs={{0,8},{4,12},{8,0},{12,4},{1,9},{5,13},{9,1},{13,5},{2,10},{6,14},... | collective-permute-start | bytes 804872 | tf_op jit(solution)/shard_map/ppermute | solution.py:39
  155.1 16.2 %collective-permute-done.10 = f32[256,262]{1,0:T(8,128)S(1)} collective-permute-done((f32[256,262]{1,0:T(8,128)S(1)}, f32[256,262]{1,0:T(8,128)S(1)}, u32[]{:S(2)}, u32[]{:S(2)}) %collective-permute-start.10) | collective-permute-done | bytes 268320 | tf_op jit(solution)/shard_map/ppermute | solution.py:39
  171.4 2.3 %gather_fusion = f32[256]{0:T(256)S(1)} fusion(f32[256,256]{1,0:T(8,128)S(1)} %slice.51, s32[256]{0:T(256)S(1)} %bitcast.78), kind=kCustom, calls=%fused_computation | custom fusion | bytes 4096 | tf_op jit(solution)/shard_map/jit(diagonal)/cond/branch_0_fun/gather | solution.py:155
  174.1 12.1 %while.77 = (s32[]{:T(128)}, f32[6,256]{1,0:T(8,128)S(1)}, f32[3,6,64]{2,1,0:T(8,128)}, s32[3,6,256]{2,1,0:T(8,128)}, f32[6,256]{1,0:T(8,128)S(1)}, /*index=5*/f...) while((s32[]{:T(128)}, f32[6,256]{1,0:T(8,128)S(1)}, f32[3,6,64]{2,1,0:T(8,128)}, ...), condition=%wide.region_8.9_spmd, body=%wide.region_2.8_spmd.sunk | while | flops 9474058 | bytes 660566 | solution.py:190
  175.2 2.2 %while.80 = (s32[]{:T(128)}, f32[6,256]{1,0:T(8,128)S(1)}, f32[6,256]{1,0:T(8,128)S(1)}, f32[6,256]{1,0:T(8,128)S(1)}, f32[6]{0:T(128)S(1)}, /*index=5*/f32[6,256]{1,0:T(8,128)S(1)}, f32[256,256]{1,0:T(8,128)S(1)}, s32[]{:T(128)}) while((s32[]{:T(128)}, f32[6,256]{1,0:T(8,128)S(1)}, f32[6,256]{1,0:T(8,128)S(1)}, f32[6,256]{1,0:T(8,128)S(1)}, ...), condition=%wide.region_7.7_spmd, body=%wide.region_4.6_spmd.sunk | while | flops 4740110 | bytes 330125 | solution.py:183
  179.2 2.2 %while.80 = (s32[]{:T(128)}, f32[6,256]{1,0:T(8,128)S(1)}, f32[6,256]{1,0:T(8,128)S(1)}, f32[6,256]{1,0:T(8,128)S(1)}, f32[6]{0:T(128)S(1)}, /*index=5*/f32[6,256]{1,0:T(8,128)S(1)}, f32[256,256]{1,0:T(8,128)S(1)}, s32[]{:T(128)}) while((s32[]{:T(128)}, f32[6,256]{1,0:T(8,128)S(1)}, f32[6,256]{1,0:T(8,128)S(1)}, f32[6,256]{1,0:T(8,128)S(1)}, ...), condition=%wide.region_7.7_spmd, body=%wide.region_4.6_spmd.sunk | while | flops 4740110 | bytes 330125 | solution.py:183
  183.3 2.2 %while.80 = (s32[]{:T(128)}, f32[6,256]{1,0:T(8,128)S(1)}, f32[6,256]{1,0:T(8,128)S(1)}, f32[6,256]{1,0:T(8,128)S(1)}, f32[6]{0:T(128)S(1)}, /*index=5*/f32[6,256]{1,0:T(8,128)S(1)}, f32[256,256]{1,0:T(8,128)S(1)}, s32[]{:T(128)}) while((s32[]{:T(128)}, f32[6,256]{1,0:T(8,128)S(1)}, f32[6,256]{1,0:T(8,128)S(1)}, f32[6,256]{1,0:T(8,128)S(1)}, ...), condition=%wide.region_7.7_spmd, body=%wide.region_4.6_spmd.sunk | while | flops 4740110 | bytes 330125 | solution.py:183
  186.2 6.4 %while.78 = (s32[]{:T(128)}, bf16[6,16384]{1,0:T(8,128)(2,1)S(1)}, bf16[6,16384]{1,0:T(8,128)(2,1)}, bf16[16,16384]{1,0:T(8,128)(2,1)S(1)}, bf16[16,16384]{1,0:T...) while((s32[]{:T(128)}, bf16[6,16384]{1,0:T(8,128)(2,1)S(1)}, ...), condition=%wide.region_10.11_spmd, body=%wide.region_9.10_spmd.sunk | while | flops 14884870 | bytes 5623963 | solution.py:211
  186.6 1.2 fusion.212
  188.2 1.2 fusion.212
  189.8 1.2 fusion.212
  191.4 1.2 fusion.212
  192.6 21.7 %all_gather.3 = bf16[6,65536]{1,0:T(8,128)(2,1)S(1)} all-gather(bf16[6,16384]{1,0:T(8,128)(2,1)S(1)} %get-tuple-element.439), channel_id=1, replica_groups=mesh['groups'=2,'cols'=4,'slab'=2,'rep'=2] {'cols'}, dimensions={1}, use_global_device_ids=true | all-gather | bytes 983040 | tf_op jit(solution)/shard_map/all_gather | solution.py:212
  214.4 1.6 reshape.112
  216.0 1.4 copy.36
  (141 shorter events, 23.8 us)
Async XLA Ops:
  0.6 15.8 %copy-start.2 = (s32[4]{0:T(128)S(1)}, s32[4]{0:T(128)}, u32[]{:S(2)}) copy-start(s32[4]{0:T(128)} %param.14) | copy-start | bytes 52
  0.6 15.9 %copy-start.1 = (bf16[6,4,256,64]{2,3,1,0:T(8,128)(2,1)S(1)}, bf16[6,4,256,64]{2,3,1,0:T(8,128)(2,1)}, u32[]{:S(2)}) copy-start(bf16[6,4,256,64]{2,3,1,0:T(8,128)(2,1)} %param.13) | copy-start | bytes 2359300
  13.4 10.1 %collective-permute-start = (bf16[4,4,1024,5]{2,3,1,0:T(8,128)(2,1)S(1)}, bf16[4,4,1024,5]{2,3,1,0:T(8,128)(2,1)S(1)}, u32[]{:S(2)}, u32[]{:S(2)}) collective-permute-start(bf16[4,4,1024,5]{2,3,1,0:T(8,128)(2,1)S(1)} %get-tuple-element.563), channel_id=1, source_target_pairs={{0,2},{2,0},{1,3},{3,1},{4,6},{6,4},{5,7},{7,5},{8,10},{10,8},{9,1... | collective-permute-start | bytes 491528 | tf_op jit(solution)/shard_map/ppermute | solution.py:24
  16.4 11.9 %collective-permute-start.1 = (bf16[4,4,1024,5]{2,3,1,0:T(8,128)(2,1)S(1)}, bf16[4,4,1024,5]{2,3,1,0:T(8,128)(2,1)S(1)}, u32[]{:S(2)}, u32[]{:S(2)}) collective-permute-start(bf16[4,4,1024,5]{2,3,1,0:T(8,128)(2,1)S(1)} %get-tuple-element.564), channel_id=1, source_target_pairs={{2,0},{0,2},{3,1},{1,3},{6,4},{4,6},{7,5},{5,7},{10,8},{8,10},{11,... | collective-permute-start | bytes 491528 | tf_op jit(solution)/shard_map/ppermute | solution.py:25
  33.8 3.5 %copy-start = (bf16[4,4,1024,266]{2,3,1,0:T(8,128)(2,1)}, bf16[4,4,1024,266]{2,3,1,0:T(8,128)(2,1)S(1)}, u32[]{:S(2)}) copy-start(bf16[4,4,1024,266]{2,3,1,0:T(8,128)(2,1)S(1)} %pad_maximum_fusion) | copy-start | bytes 26148868
  38.5 4.6 %collective-permute-start.2 = (bf16[4,4,5,266]{3,1,2,0:T(4,128)(2,1)S(1)}, bf16[4,4,5,266]{3,1,2,0:T(4,128)(2,1)S(1)}, u32[]{:S(2)}, u32[]{:S(2)}) collective-permute-start(bf16[4,4,5,266]{3,1,2,0:T(4,128)(2,1)S(1)} %copy.27), channel_id=1, source_target_pairs={{0,1},{1,0},{2,3},{3,2},{4,5},{5,4},{6,7},{7,6},{8,9},{9,8},{10,11... | collective-permute-start | bytes 127688 | tf_op jit(solution)/shard_map/ppermute | solution.py:24
  39.1 4.6 %collective-permute-start.3 = (bf16[4,4,5,266]{3,1,2,0:T(4,128)(2,1)S(1)}, bf16[4,4,5,266]{3,1,2,0:T(4,128)(2,1)S(1)}, u32[]{:S(2)}, u32[]{:S(2)}) collective-permute-start(bf16[4,4,5,266]{3,1,2,0:T(4,128)(2,1)S(1)} %copy.28), channel_id=1, source_target_pairs={{1,0},{0,1},{3,2},{2,3},{5,4},{4,5},{7,6},{6,7},{9,8},{8,9},{11,10... | collective-permute-start | bytes 127688 | tf_op jit(solution)/shard_map/ppermute | solution.py:25
  89.4 12.2 %collective-permute-start.4 = (bf16[2,4,16384]{2,1,0:T(4,128)(2,1)S(1)}, bf16[2,4,16384]{2,1,0:T(4,128)(2,1)S(1)}, u32[]{:S(2)}, u32[]{:S(2)}) collective-permute-start(bf16[2,4,16384]{2,1,0:T(4,128)(2,1)S(1)} %get-tuple-element.569), channel_id=1, source_target_pairs={{0,4},{4,0},{8,12},{12,8},{1,5},{5,1},{9,13},{13,9},{2,6},{6,2},{1... | collective-permute-start | bytes 786440 | tf_op jit(solution)/shard_map/ppermute | solution.py:125
  92.9 21.3 %collective-permute-start.5 = (bf16[2,4,16384]{2,1,0:T(4,128)(2,1)S(1)}, bf16[2,4,16384]{2,1,0:T(4,128)(2,1)S(1)}, u32[]{:S(2)}, u32[]{:S(2)}) collective-permute-start(bf16[2,4,16384]{2,1,0:T(4,128)(2,1)S(1)} %get-tuple-element.570), channel_id=1, source_target_pairs={{0,8},{4,12},{8,0},{12,4},{1,9},{5,13},{9,1},{13,5},{2,10},{6,14},... | collective-permute-start | bytes 786440 | tf_op jit(solution)/shard_map/ppermute | solution.py:125
  95.5 18.9 %collective-permute-start.6 = (bf16[2,4,16384]{2,1,0:T(4,128)(2,1)S(1)}, bf16[2,4,16384]{2,1,0:T(4,128)(2,1)S(1)}, u32[]{:S(2)}, u32[]{:S(2)}) collective-permute-start(bf16[2,4,16384]{2,1,0:T(4,128)(2,1)S(1)} %get-tuple-element.567), channel_id=1, source_target_pairs={{0,12},{4,8},{8,4},{12,0},{1,13},{5,9},{9,5},{13,1},{2,14},{6,10},... | collective-permute-start | bytes 786440 | tf_op jit(solution)/shard_map/ppermute | solution.py:125
  125.7 1.8 collective-permute-start.7
  127.5 11.2 %collective-permute-start.8 = (f32[256,262]{1,0:T(8,128)S(1)}, f32[256,262]{1,0:T(8,128)S(1)}, u32[]{:S(2)}, u32[]{:S(2)}) collective-permute-start(f32[256,262]{1,0:T(8,128)S(1)} %fusion.186), channel_id=1, source_target_pairs={{0,2},{2,0},{1,3},{3,1},{4,6},{6,4},{5,7},{7,5},{8,10},{10,8},{9,1... | collective-permute-start | bytes 804872 | tf_op jit(solution)/shard_map/ppermute | solution.py:39
  138.8 13.4 %collective-permute-start.9 = (f32[256,262]{1,0:T(8,128)S(1)}, f32[256,262]{1,0:T(8,128)S(1)}, u32[]{:S(2)}, u32[]{:S(2)}) collective-permute-start(f32[256,262]{1,0:T(8,128)S(1)} %add.219), channel_id=1, source_target_pairs={{0,4},{4,0},{8,12},{12,8},{1,5},{5,1},{9,13},{13,9},{2,6},{6,2},{1... | collective-permute-start | bytes 804872 | tf_op jit(solution)/shard_map/ppermute | solution.py:39
  152.2 19.1 %collective-permute-start.10 = (f32[256,262]{1,0:T(8,128)S(1)}, f32[256,262]{1,0:T(8,128)S(1)}, u32[]{:S(2)}, u32[]{:S(2)}) collective-permute-start(f32[256,262]{1,0:T(8,128)S(1)} %add.220), channel_id=1, source_target_pairs={{0,8},{4,12},{8,0},{12,4},{1,9},{5,13},{9,1},{13,5},{2,10},{6,14},... | collective-permute-start | bytes 804872 | tf_op jit(solution)/shard_map/ppermute | solution.py:39
